TPU v7x, 128 devices: a whole 4x4x4 slice. The times are simulated.
128 devices in a mesh: req: 16 (over z, x), mlp: 8 (over y, core).
Axes of the slice: x: 4, y: 4, z: 4, core: 2. Of those that a mesh axis runs over, the one named last changes fastest.
Arguments:
- residual_input: bfloat16 [9216, 5120], P('req', 'mlp'), as said below
- attention_output: bfloat16 [9216, 3072], P('req', 'mlp'), may hold values from -6 to 6
- request_length: int32 [16, 4], replicated, may hold values from 1 to 573, as said below
- request_group: int32 [64], replicated, may hold values from 0 to 7
- adapter_per_group: int32 [8], replicated, may hold values from 0 to 15
- output_weight: bfloat16 [3072, 5120], P('mlp', 'req'), may hold values from -0.109375 to 0.109375
- output_down_maps: bfloat16 [3072, 16, 16], P('mlp'), may hold values from -0.109375 to 0.109375
- output_up_maps: bfloat16 [16, 16, 5120], P(None, None, 'mlp'), may hold values from -1.5 to 1.5
- modulation: float32 [8, 3, 5120], replicated, may hold values from -3 to 3
- hidden_down_maps: bfloat16 [5120, 16, 16], P('mlp'), may hold values from -0.078125 to 0.078125
- hidden_up_maps: bfloat16 [16, 16, 6912], P(None, None, 'mlp'), may hold values from -1.5 to 1.5
- up_weight: bfloat16 [5120, 6912], P('req', 'mlp'), may hold values from -0.078125 to 0.078125
- down_weight: bfloat16 [6912, 5120], P('mlp', 'req'), may hold values from -0.078125 to 0.078125
Outputs:
- layer_out: bfloat16 [384, 16, 5120], P(None, 'req', 'mlp')
Inputs may be any that keep to these rules, and one draw needn't show every extreme that they name: `request_length`: the 4 lengths of one block sum to at most 576, and to exactly 576 for one block; all lengths together sum to 6144. One request has exactly the largest length. `residual_input`: rows of a block past its live rows are never read.
All inputs are finite; a program needn't handle non-finite values.
Results may differ from a plain program's by a relative error of at most 0.012.
Values may be sent and summed in bfloat16 or wider, within the bound.
No kernel may reach another device: no remote copies, remote signals or barrier semaphores. Data moves between devices by JAX's collectives and lax.ppermute only.
A program may use at most 192 MiB of HBM per device.

v0:
```python
import jax
import jax.numpy as jnp
from jax import lax
from jax.sharding import PartitionSpec as P

MODEL_WIDTH = 5120
ADAPTER_RANK = 16
ADAPTER_TOTAL = 16
TOK_DEV = 384
CAP = 576
norm_epsilon = 1e-06


def send_layout(packed, offset, req_count):
    shaped = packed.reshape(packed.shape[0] // req_count, req_count, packed.shape[1])
    return jnp.roll(shaped, offset, axis=1)


def compact(moved, starts, ends, req_count, device_index):
    slots = moved.shape[0] * moved.shape[1]
    flat_rows = moved.reshape(slots, moved.shape[2])
    token_rank = jnp.arange(TOK_DEV, dtype=jnp.int32) * req_count + device_index
    source = jnp.sum((ends[None, :] <= token_rank[:, None]).astype(jnp.int32), axis=1)
    source_hot = source[:, None] == jnp.arange(req_count, dtype=jnp.int32)[None, :]
    source_start = jnp.sum(jnp.where(source_hot, starts[None, :], 0), axis=1)
    position = (token_rank - source_start) // req_count * req_count + source
    return jnp.take(flat_rows, position, axis=0)


def token_tables(token_rank, request_length, request_group, adapter_per_group, modulation):
    req_ends = jnp.cumsum(request_length.reshape(-1))
    request_count = req_ends.shape[0]
    request = jnp.sum((req_ends[None, :] <= token_rank[:, None]).astype(jnp.int32), axis=1)
    request = jnp.minimum(request, request_count - 1)
    request_hot = request[:, None] == jnp.arange(request_count, dtype=jnp.int32)[None, :]
    group_ids = jnp.sum(jnp.where(request_hot, request_group[None, :], 0), axis=1)
    group_count = adapter_per_group.shape[0]
    group_hot = group_ids[:, None] == jnp.arange(group_count, dtype=jnp.int32)[None, :]
    adapter_of_row = jnp.sum(jnp.where(group_hot, adapter_per_group[None, :], 0), axis=1)
    adapter_hot = (
        adapter_of_row[:, None] == jnp.arange(ADAPTER_TOTAL, dtype=jnp.int32)[None, :]
    ).astype(jnp.float32)
    mod_rows = jnp.dot(
        group_hot.astype(jnp.float32),
        modulation.reshape(group_count, -1),
        precision=lax.Precision.HIGHEST,
    )
    return (adapter_hot, mod_rows.reshape(token_rank.shape[0], 3, modulation.shape[2]))


def select_low(output_rank_rows, adapter_hot):
    shaped = output_rank_rows.reshape(output_rank_rows.shape[0], ADAPTER_TOTAL, ADAPTER_RANK)
    return jnp.sum(shaped * adapter_hot[:, :, None], axis=1)


def expand_rank_rows(low_rows, adapter_hot):
    spread_rows = adapter_hot.astype(jnp.bfloat16)[:, :, None] * low_rows[:, None, :]
    return spread_rows.reshape(low_rows.shape[0], ADAPTER_TOTAL * ADAPTER_RANK)


def layer_rows(
    attention_rows,
    residual_rows,
    token_rank,
    request_length,
    request_group,
    adapter_per_group,
    output_weight,
    output_down_maps,
    output_up_maps,
    modulation,
    hidden_down_maps,
    hidden_up_maps,
    up_weight,
    down_weight,
):
    column_index = lax.axis_index("mlp")
    shard_hidden_width = residual_rows.shape[1]
    adapter_hot, mod_rows = token_tables(
        token_rank, request_length, request_group, adapter_per_group, modulation
    )
    shift_rows = mod_rows[:, 0]
    scale_rows = mod_rows[:, 1]
    gate_rows = lax.dynamic_slice_in_dim(
        mod_rows[:, 2], column_index * shard_hidden_width, shard_hidden_width, 1
    )
    head_terms = jnp.dot(
        attention_rows,
        lax.all_gather(output_weight, "req", axis=1, tiled=True),
        preferred_element_type=jnp.float32,
    )
    projection_rows = lax.psum_scatter(
        head_terms.astype(jnp.bfloat16), "mlp", scatter_dimension=1, tiled=True
    ).astype(jnp.float32)
    output_rank_rows = jnp.dot(
        attention_rows,
        output_down_maps.reshape(attention_rows.shape[1], ADAPTER_TOTAL * ADAPTER_RANK),
        preferred_element_type=jnp.float32,
    )
    output_rank_values = lax.psum(
        select_low(output_rank_rows, adapter_hot).astype(jnp.bfloat16), "mlp"
    )
    adapter_delta = jnp.dot(
        expand_rank_rows(output_rank_values, adapter_hot),
        output_up_maps.reshape(ADAPTER_TOTAL * ADAPTER_RANK, shard_hidden_width),
        preferred_element_type=jnp.float32,
    )
    blended_rows = (residual_rows.astype(jnp.float32) + projection_rows + adapter_delta).astype(
        jnp.bfloat16
    )
    values = blended_rows.astype(jnp.float32)
    full_rows = lax.all_gather(blended_rows, "mlp", axis=1, tiled=True).astype(jnp.float32)
    row_mean = jnp.sum(full_rows, axis=1, keepdims=True) / MODEL_WIDTH
    variance = (
        jnp.sum(full_rows * full_rows, axis=1, keepdims=True) / MODEL_WIDTH - row_mean * row_mean
    )
    normalized_rows = (
        (full_rows - row_mean) * lax.rsqrt(variance + norm_epsilon) * (1.0 + scale_rows)
        + shift_rows
    ).astype(jnp.bfloat16)
    normed_local = lax.dynamic_slice_in_dim(
        normalized_rows, column_index * shard_hidden_width, shard_hidden_width, 1
    )
    part_low = jnp.dot(
        normed_local,
        hidden_down_maps.reshape(shard_hidden_width, ADAPTER_TOTAL * ADAPTER_RANK),
        preferred_element_type=jnp.float32,
    )
    hidden_rank_values = lax.psum(select_low(part_low, adapter_hot).astype(jnp.bfloat16), "mlp")
    hidden_unit_width = up_weight.shape[1]
    hidden_total = jnp.dot(
        normalized_rows,
        lax.all_gather(up_weight, "req", axis=0, tiled=True),
        preferred_element_type=jnp.float32,
    )
    hidden_total = hidden_total + jnp.dot(
        expand_rank_rows(hidden_rank_values, adapter_hot),
        hidden_up_maps.reshape(ADAPTER_TOTAL * ADAPTER_RANK, hidden_unit_width),
        preferred_element_type=jnp.float32,
    )
    hidden = jax.nn.gelu(hidden_total, approximate=True).astype(jnp.bfloat16)
    down_terms = jnp.dot(
        hidden,
        lax.all_gather(down_weight, "req", axis=1, tiled=True),
        preferred_element_type=jnp.float32,
    )
    down_sum = lax.psum_scatter(
        down_terms.astype(jnp.bfloat16), "mlp", scatter_dimension=1, tiled=True
    ).astype(jnp.float32)
    return (values + gate_rows * down_sum).astype(jnp.bfloat16)


def local(
    residual_input,
    attention_output,
    request_length,
    request_group,
    adapter_per_group,
    output_weight,
    output_down_maps,
    output_up_maps,
    modulation,
    hidden_down_maps,
    hidden_up_maps,
    up_weight,
    down_weight,
):
    req_count = lax.axis_size("req")
    device_index = lax.axis_index("req")
    live_rows = jnp.sum(request_length, axis=1)
    dev_ends = jnp.cumsum(live_rows)
    dev_starts = dev_ends - live_rows
    offset = dev_starts[device_index]
    shard_hidden_width = residual_input.shape[1]
    weights = (
        request_length,
        request_group,
        adapter_per_group,
        output_weight,
        output_down_maps,
        output_up_maps,
        modulation,
        hidden_down_maps,
        hidden_up_maps,
        up_weight,
        down_weight,
    )
    token_rank = jnp.minimum(offset + jnp.arange(CAP, dtype=jnp.int32), TOK_DEV * req_count - 1)
    packed_out = layer_rows(attention_output, residual_input, token_rank, *weights)
    moved_out = lax.all_to_all(
        send_layout(packed_out, offset, req_count), "req", split_axis=1, concat_axis=1, tiled=True
    )
    result = compact(moved_out, dev_starts, dev_ends, req_count, device_index)
    return result.reshape(TOK_DEV, 1, shard_hidden_width)


def solution(mesh):
    placed = (
        P("req", "mlp"),
        P("req", "mlp"),
        P(),
        P(),
        P(),
        P("mlp", "req"),
        P("mlp", None, None),
        P(None, None, "mlp"),
        P(),
        P("mlp", None, None),
        P(None, None, "mlp"),
        P("req", "mlp"),
        P("mlp", "req"),
    )
    return jax.shard_map(
        local, mesh=mesh, in_specs=placed, out_specs=P(None, "req", "mlp"), check_vma=False
    )
```

profile of v0, /device:TPU:9, one launch (start us, length us, event | category | flops | bytes accessed | tf_op | source)
XLA Modules:
  0.0 418.9 jit_solution(15654548941162831555)
XLA Ops:
  6.5 0.7 all-gather.5.cloned.1.call-update
  7.3 54.6 %all-gather.5.cloned.1.call-done = bf16[384,5120]{0,1:T(8,128)(2,1)} async-done(((bf16[384,320]{0,1:T(8,128)(2,1)}), bf16[384,5120]{0,1:T(8,128)(2,1)}) %all-gather.5.cloned.1.call-update) | async-done | bytes 3932176 | tf_op jit(solution)/shard_map/all_gather | solution.py:89
  61.9 8.1 %convolution_convert_fusion.1 = bf16[576,5120]{1,0:T(8,128)(2,1)} fusion(bf16[576,384]{1,0:T(8,128)(2,1)} %param.14, bf16[384,5120]{0,1:T(8,128)(2,1)} %all-gather.5.cloned.1.call-done), kind=kOutput, calls=%fused_computation.13 | convolution fusion | flops 2267873280 | bytes 10272768 | tf_op jit(solution)/shard_map/dot_general | solution.py:87
  70.0 8.6 %copy.34 = bf16[576,5120]{0,1:T(8,128)(2,1)} copy(bf16[576,5120]{1,0:T(8,128)(2,1)} %convolution_convert_fusion.1) | data formatting | bytes 11796480
  78.7 0.6 copy-done.5
  79.3 0.1 copy.29
  79.4 0.1 copy.28
  79.5 0.1 reduce
  79.7 0.1 reduce-window.16
  79.8 0.1 reduce.1
  79.9 0.6 dynamic_slice.15
  80.5 0.6 add_minimum_fusion
  81.2 0.1 convert_reduce_fusion.1
  81.3 0.1 select_reduce_fusion
  81.4 0.1 select_reduce_fusion.2
  81.5 0.4 fusion.18
  81.9 20.7 %psum.14 = bf16[576,16]{0,1:T(8,128)(2,1)S(1)} all-reduce(bf16[576,16]{0,1:T(8,128)(2,1)S(1)} %fusion.18), channel_id=1, replica_groups=mesh['req'=16,'mlp'=8] {'mlp'}, use_global_device_ids=true, to_apply=%region_10.11 | all-reduce | flops 9216 | bytes 36864 | tf_op jit(solution)/shard_map/psum | solution.py:100
  102.6 19.1 %reduce-scatter.7.cloned.1.call-done = bf16[640,576]{1,0:T(8,128)(2,1)} async-done(((bf16[5120,576]{1,0:T(8,128)(2,1)}), bf16[640,576]{1,0:T(8,128)(2,1)}) %reduce-scatter.7.cloned.1.call-update) | async-done | bytes 737296
  121.8 1.5 copy.35
  123.3 1.3 fusion.16
  124.6 0.5 all-gather.9.cloned.1.call-update
  125.2 0.5 all-gather.11.cloned.1.call-update
  125.8 0.2 reduce-scatter.9.cloned.1.call-start
  126.0 18.4 %fusion.22 = f32[576,3,5120]{2,0,1:T(8,128)} fusion(f32[8,3,5120]{2,0,1:T(8,128)S(1)} %copy-done, s32[576]{0:T(1024)S(1)} %select_reduce_fusion), kind=kOutput, calls=%fused_computation.38 | convolution fusion | flops 849351168 | bytes 35883264 | tf_op jit(solution)/shard_map/dot_general | solution.py:43
  144.4 19.8 %all-gather.7.cloned.1.call-done = bf16[576,5120]{1,0:T(8,128)(2,1)} async-done(((bf16[576,640]{1,0:T(8,128)(2,1)}), bf16[576,5120]{1,0:T(8,128)(2,1)}) %all-gather.7.cloned.1.call-update) | async-done | bytes 5898256 | tf_op jit(solution)/shard_map/all_gather | solution.py:112
  164.2 4.6 %convert_reduce_fusion = (f32[576]{0:T(1024)S(1)}, f32[576]{0:T(1024)S(1)}) fusion(bf16[576,5120]{1,0:T(8,128)(2,1)} %all-gather.7.cloned.1.call-done), kind=kLoop, calls=%fused_computation.3 | loop fusion | flops 11795328 | bytes 5902848 | tf_op jit(solution)/shard_map/reduce_sum | solution.py:113
  168.8 9.6 %fusion.3 = bf16[576,5120]{1,0:T(8,128)(2,1)S(1)} fusion(bf16[576,5120]{1,0:T(8,128)(2,1)S(1)} %copy-done.2, f32[576,3,5120]{2,0,1:T(8,128)} %fusion.22, f32[576]{0:T(1024)S(1)} %get-tuple-element.8, f32[576]{0:T(1024)S(1)} %get-tuple-element.7), kind=kLoop, calls=%fused_computation.7 | loop fusion | flops 20643840 | bytes 35394048 | tf_op jit(solution)/shard_map/convert_element_type | solution.py:120
  178.5 2.5 copy-done.3
  181.0 0.5 fusion.17
  181.4 20.5 %psum.15 = bf16[576,16]{0,1:T(8,128)(2,1)S(1)} all-reduce(bf16[576,16]{0,1:T(8,128)(2,1)S(1)} %fusion.17), channel_id=1, replica_groups=mesh['req'=16,'mlp'=8] {'mlp'}, use_global_device_ids=true, to_apply=%region_14.15 | all-reduce | flops 9216 | bytes 36864 | tf_op jit(solution)/shard_map/psum | solution.py:129
  202.0 39.1 %all-gather.9.cloned.1.call-done = bf16[5120,864]{1,0:T(8,128)(2,1)} async-done(((bf16[320,864]{1,0:T(8,128)(2,1)}), bf16[5120,864]{1,0:T(8,128)(2,1)}) %all-gather.9.cloned.1.call-update) | async-done | bytes 8847376 | tf_op jit(solution)/shard_map/all_gather | solution.py:133
  241.1 11.9 %fusion.44 = f32[576,864]{1,0:T(8,128)} fusion(bf16[576,5120]{1,0:T(8,128)(2,1)} %copy-done.3, bf16[5120,864]{1,0:T(8,128)(2,1)} %all-gather.9.cloned.1.call-done), kind=kOutput, calls=%fused_computation.87 | convolution fusion | flops 5096079360 | bytes 16736256 | tf_op jit(solution)/shard_map/dot_general | solution.py:131
  253.0 64.2 %all-gather.11.cloned.1.call-done = bf16[864,5120]{0,1:T(8,128)(2,1)} async-done(((bf16[864,320]{0,1:T(8,128)(2,1)}), bf16[864,5120]{0,1:T(8,128)(2,1)}) %all-gather.11.cloned.1.call-update) | async-done | bytes 8847376 | tf_op jit(solution)/shard_map/all_gather | solution.py:144
  317.2 12.2 %convolution_convert_fusion = bf16[576,5120]{1,0:T(8,128)(2,1)} fusion(bf16[864,5120]{0,1:T(8,128)(2,1)} %all-gather.11.cloned.1.call-done, f32[576,864]{1,0:T(8,128)} %fusion.44, bf16[16,16,864]{2,1,0:T(8,128)(2,1)S(1)} %copy-done.9, bf16[576,16]{0,1:T(8,128)(2,1)S(1)} %psum.15, bf16[576,16]{0,1:T(8,128)(2,1)S(1)} %get-tuple-element.9), kind=kOutput, calls=%fused_computation.12 | convolution fusion | flops 5358956544 | bytes 17215488 | tf_op jit(solution)/shard_map/dot_general | solution.py:142
  329.4 8.6 %copy.36 = bf16[576,5120]{0,1:T(8,128)(2,1)} copy(bf16[576,5120]{1,0:T(8,128)(2,1)} %convolution_convert_fusion) | data formatting | bytes 11796480
  338.0 10.4 %slice.14 = f32[576,1,5120]{2,0,1:T(8,128)} slice(f32[576,3,5120]{2,0,1:T(8,128)} %fusion.22), slice={[0:576], [2:3], [0:5120]} | slice | bytes 23592960 | tf_op jit(solution)/shard_map/slice | solution.py:85
  350.3 30.5 %reduce-scatter.9.cloned.1.call-done = bf16[640,576]{1,0:T(8,128)(2,1)} async-done(((bf16[5120,576]{1,0:T(8,128)(2,1)}), bf16[640,576]{1,0:T(8,128)(2,1)}) %reduce-scatter.9.cloned.1.call-update) | async-done | bytes 737296
  380.8 1.5 copy.37
  382.3 1.6 fusion.15
  383.9 0.1 copy.31
  384.1 1.3 fusion.19
  385.3 6.7 %all-to-all-start = ((bf16[36,16,640]{2,0,1:T(8,128)(2,1)}), bf16[36,16,640]{2,0,1:T(8,128)(2,1)S(1)}, u32[]{:S(2)}, u32[]{:S(2)}) async-start(bf16[36,16,640]{2,0,1:T(8,128)(2,1)} %fusion.19), calls=%async_computation | async-start | bytes 1638400 | tf_op jit(solution)/shard_map/all_to_all | solution.py:190
  392.0 0.1 convert_reduce_fusion.2
  392.1 0.1 select_reduce_fusion.1
  392.3 16.5 %all-to-all-done = bf16[36,16,640]{2,0,1:T(8,128)(2,1)S(1)} async-done(((bf16[36,16,640]{2,0,1:T(8,128)(2,1)}), bf16[36,16,640]{2,0,1:T(8,128)(2,1)S(1)}, u32[]{:S(2)}, u32[]{:S(2)}) %all-to-all-start) | async-done | bytes 737312 | tf_op jit(solution)/shard_map/all_to_all | solution.py:190
  408.8 0.1 copy.33
  408.9 2.2 gather_fusion
  411.1 0.9 bitcast_select_fusion
  (45 shorter events, 0.5 us)
Async XLA Ops:
  6.5 119.5 %copy-start = (f32[8,3,5120]{2,0,1:T(8,128)S(1)}, f32[8,3,5120]{2,0,1:T(8,128)}, u32[]{:S(2)}) copy-start(f32[8,3,5120]{2,0,1:T(8,128)} %param.21) | copy-start | bytes 1474564
  6.5 55.4 %all-gather.5.cloned.1.call-start = ((), (), s32[]{:S(2)}) async-start(), calls=%async_computation.3 | async-start | bytes 4177920 | tf_op jit(solution)/shard_map/all_gather | solution.py:89
  7.3 114.5 %reduce-scatter.7.cloned.1.call-start = ((), (), s32[]{:S(2)}) async-start(), calls=%async_computation.7 | async-start | bytes 7372800
  78.6 0.7 copy-start.5
  78.6 2.7 copy-start.6
  78.6 2.8 copy-start.7
  78.6 2.9 copy-start.10
  78.6 2.9 copy-start.13
  78.6 44.6 %copy-start.8 = (bf16[576,640]{1,0:T(8,128)(2,1)S(1)}, bf16[576,640]{1,0:T(8,128)(2,1)}, u32[]{:S(2)}) copy-start(bf16[576,640]{1,0:T(8,128)(2,1)} %param.13) | copy-start | bytes 2211844
  78.7 44.6 %copy-start.11 = (bf16[16,16,640]{2,1,0:T(8,128)(2,1)S(1)}, bf16[16,16,640]{2,1,0:T(8,128)(2,1)}, u32[]{:S(2)}) copy-start(bf16[16,16,640]{2,1,0:T(8,128)(2,1)} %param.20) | copy-start | bytes 983044
  78.7 85.5 %all-gather.7.cloned.1.call-start = ((), (), s32[]{:S(2)}) async-start(), calls=%async_computation.4 | async-start | bytes 6635520 | tf_op jit(solution)/shard_map/all_gather | solution.py:112
  124.6 116.5 %all-gather.9.cloned.1.call-start = ((), (), s32[]{:S(2)}) async-start(), calls=%async_computation.5 | async-start | bytes 9748480 | tf_op jit(solution)/shard_map/all_gather | solution.py:133
  125.2 192.0 %all-gather.11.cloned.1.call-start = ((), (), s32[]{:S(2)}) async-start(), calls=%async_computation.6 | async-start | bytes 9748480 | tf_op jit(solution)/shard_map/all_gather | solution.py:144
  125.8 255.0 %reduce-scatter.9.cloned.1.call-start = ((), (), s32[]{:S(2)}) async-start(), calls=%async_computation.8 | async-start | bytes 7372800
  164.2 4.6 %copy-start.2 = (bf16[576,5120]{1,0:T(8,128)(2,1)S(1)}, bf16[576,5120]{1,0:T(8,128)(2,1)}, u32[]{:S(2)}) copy-start(bf16[576,5120]{1,0:T(8,128)(2,1)} %all-gather.7.cloned.1.call-done) | copy-start | bytes 17694724
  168.8 12.1 %copy-start.12 = (bf16[640,16,16]{0,2,1:T(8,128)(2,1)S(1)}, bf16[640,16,16]{0,2,1:T(8,128)(2,1)}, u32[]{:S(2)}) copy-start(bf16[640,16,16]{0,2,1:T(8,128)(2,1)} %param.22) | copy-start | bytes 983044
  178.5 2.5 copy-start.3
  202.0 115.2 %copy-start.9 = (bf16[16,16,864]{2,1,0:T(8,128)(2,1)S(1)}, bf16[16,16,864]{2,1,0:T(8,128)(2,1)}, u32[]{:S(2)}) copy-start(bf16[16,16,864]{2,1,0:T(8,128)(2,1)} %param.23) | copy-start | bytes 1327108
  338.0 44.3 %copy-start.4 = (bf16[576,640]{1,0:T(8,128)(2,1)S(1)}, bf16[576,640]{1,0:T(8,128)(2,1)}, u32[]{:S(2)}) copy-start(bf16[576,640]{1,0:T(8,128)(2,1)} %fusion.16) | copy-start | bytes 2211844
  383.9 28.1 %copy-start.1 = (f32[8,3,5120]{2,0,1:T(8,128)S(1)}, f32[8,3,5120]{2,0,1:T(8,128)}, u32[]{:S(2)}) copy-start(f32[8,3,5120]{2,0,1:T(8,128)} %param.21) | copy-start | bytes 1474564
  385.3 23.5 %all-to-all-start = ((bf16[36,16,640]{2,0,1:T(8,128)(2,1)}), bf16[36,16,640]{2,0,1:T(8,128)(2,1)S(1)}, u32[]{:S(2)}, u32[]{:S(2)}) async-start(bf16[36,16,640]{2,0,1:T(8,128)(2,1)} %fusion.19), calls=%async_computation | async-start | bytes 1638400 | tf_op jit(solution)/shard_map/all_to_all | solution.py:190
Sparse Core Ops, SparseCore 0:
  9.5 52.4 all-gather.4
  78.8 42.9 reduce-scatter.6
  124.7 39.4 all-gather.6
  166.2 74.9 all-gather.8
  243.1 74.0 all-gather.10
  338.1 42.6 reduce-scatter.8
where the time goes:
time: 420 us; the launch traced here: 419 us
  waiting for transfers between devices  246 us (59%)
  matrix products  52.6 us (13%)
  blocking collectives  41.2 us (10%)
  local copies, waits for them, and re-layouts  37 us (9%)
  other arithmetic  19.6 us (5%)
  between operations  15.7 us (4%)
  starting transfers between devices  7.06 us (2%)
    all_gather x1, waiting for transfers between devices, layer_rows(): lax.all_gather(down_weight, 'req', axis=1, tiled=True)  64.2 us
    all_gather x1, waiting for transfers between devices, layer_rows(): lax.all_gather(output_weight, 'req', axis=1, tiled=True)  54.6 us
    unnamed x8, waiting for transfers between devices  51.4 us
    all_gather x1, waiting for transfers between devices, layer_rows(): lax.all_gather(up_weight, 'req', axis=0, tiled=True)  39.1 us
    unnamed x33, local copies, waits for them, and re-layouts  23.4 us
    psum x1, blocking collectives, layer_rows(): lax.psum(select_low(output_rank_rows, adapter_hot).astype(jnp.bfloat16),...  20.7 us
    psum x1, blocking collectives, layer_rows(): lax.psum(select_low(part_low, adapter_hot).astype(jnp.bfloat16), 'mlp')  20.5 us
    all_gather x1, waiting for transfers between devices, layer_rows(): lax.all_gather(blended_rows, 'mlp', axis=1, tiled=True).astype(jnp.float32)  19.8 us
  transfers between devices with their start and end apart: 7, of which 7 were waited for; matrix products, arithmetic and copies ran while one was open for 14% of the time, Pallas kernels for 0%

commit v1 on v0

--- a/solution.py
+++ b/solution.py
@@ -9,6 +9,24 @@
 TOK_DEV = 384
 CAP = 576
 norm_epsilon = 1e-06
+
+
+def gather_around(array, axis, dim):
+    ways, here, step = (lax.axis_size(axis), lax.axis_index(axis), array.shape[dim])
+    dims = [n * ways if d == dim else n for d, n in enumerate(array.shape)]
+    full = lax.dynamic_update_slice_in_dim(
+        jnp.zeros(dims, array.dtype), array, here * step, axis=dim
+    )
+    going_up = going_down = array
+    for far in range(1, ways // 2 + 1):
+        going_up = lax.ppermute(going_up, axis, [(d, (d + 1) % ways) for d in range(ways)])
+        full = lax.dynamic_update_slice_in_dim(full, going_up, (here - far) % ways * step, axis=dim)
+        if 2 * far < ways:
+            going_down = lax.ppermute(going_down, axis, [(d, (d - 1) % ways) for d in range(ways)])
+            full = lax.dynamic_update_slice_in_dim(
+                full, going_down, (here + far) % ways * step, axis=dim
+            )
+    return full
 
 
 def send_layout(packed, offset, req_count):
@@ -109,7 +127,7 @@
         jnp.bfloat16
     )
     values = blended_rows.astype(jnp.float32)
-    full_rows = lax.all_gather(blended_rows, "mlp", axis=1, tiled=True).astype(jnp.float32)
+    full_rows = gather_around(blended_rows, "mlp", 1).astype(jnp.float32)
     row_mean = jnp.sum(full_rows, axis=1, keepdims=True) / MODEL_WIDTH
     variance = (
         jnp.sum(full_rows * full_rows, axis=1, keepdims=True) / MODEL_WIDTH - row_mean * row_mean

time: 420 us -> 376 us (0.90)
  waiting for transfers between devices: 246 us -> 176 us
  local copies, waits for them, and re-layouts: 37 us -> 49 us
  starting transfers between devices: 7.06 us -> 14.2 us
  blocking collectives: 41.2 us -> 47.5 us
    all_gather x1, waiting for transfers between devices: 39.1 us -> 0.02 us  [layer_rows(): lax.all_gather(up_weight, 'req', axis=0, tiled=True)]
    all_gather x1, waiting for transfers between devices: 64.2 us -> 36.4 us  [layer_rows(): lax.all_gather(down_weight, 'req', axis=1, tiled=True)]
    all_gather x1 -> x0, waiting for transfers between devices: 19.8 us -> none  [layer_rows(): lax.all_gather(blended_rows, 'mlp', axis=1, tiled=True).astype(jnp.float32)]
    ppermute x0 -> x7, waiting for transfers between devices: none -> 17.7 us  [the longest x4 16.6 us: gather_around(): lax.ppermute(going_up, axis, [(d, (d + 1) % ways) for d in range(ways)])]
    dynamic_update_slice x0 -> x7, local copies, waits for them, and re-layouts: none -> 9.22 us  [the longest x4 5.13 us: gather_around(): lax.dynamic_update_slice_in_dim(full, going_up, (here - far) % ways * ste...]
    ppermute x0 -> x7, starting transfers between devices: none -> 7.36 us  [the longest x4 7.35 us: gather_around(): lax.ppermute(going_up, axis, [(d, (d + 1) % ways) for d in range(ways)])]
    psum x1, blocking collectives: 20.5 us -> 26.8 us  [layer_rows(): lax.psum(select_low(part_low, adapter_hot).astype(jnp.bfloat16), 'mlp')]
    unnamed x8 -> x7, waiting for transfers between devices: 51.4 us -> 50.7 us
  transfers between devices with their start and end apart: 7 -> 13, of which waited for: 7 -> 10; matrix products, arithmetic and copies ran while one was open for 14% -> 20% of each run, Pallas kernels for 0% -> 0%
where the time goes in v1:
time: 376 us; the launch traced here: 375 us
  waiting for transfers between devices  176 us (47%)
  matrix products  51.8 us (14%)
  local copies, waits for them, and re-layouts  49 us (13%)
  blocking collectives  47.5 us (13%)
  other arithmetic  21.4 us (6%)
  between operations  15.4 us (4%)
  starting transfers between devices  14.2 us (4%)
    all_gather x1, waiting for transfers between devices, layer_rows(): lax.all_gather(output_weight, 'req', axis=1, tiled=True)  54.6 us
    unnamed x7, waiting for transfers between devices  50.7 us
    all_gather x1, waiting for transfers between devices, layer_rows(): lax.all_gather(down_weight, 'req', axis=1, tiled=True)  36.4 us
    psum x1, blocking collectives, layer_rows(): lax.psum(select_low(part_low, adapter_hot).astype(jnp.bfloat16), 'mlp')  26.8 us
    unnamed x33, local copies, waits for them, and re-layouts  23 us
    psum x1, blocking collectives, layer_rows(): lax.psum(select_low(output_rank_rows, adapter_hot).astype(jnp.bfloat16),...  20.7 us
    dot_general x1, matrix products, token_tables(): jnp.dot(group_hot.astype(jnp.float32), modulation.reshape(group_count, -1...  18.2 us
    ppermute x4, waiting for transfers between devices, gather_around(): lax.ppermute(going_up, axis, [(d, (d + 1) % ways) for d in range(ways)])  16.6 us
  transfers between devices with their start and end apart: 13, of which 10 were waited for; matrix products, arithmetic and copies ran while one was open for 20% of the time, Pallas kernels for 0%

profile of v1, /device:TPU:9, one launch (start us, length us, event | category | flops | bytes accessed | tf_op | source)
XLA Modules:
  0.0 375.0 jit_solution(7013035820116279319)
XLA Ops:
  6.5 0.7 all-gather.4.cloned.1.call-update
  7.3 54.6 %all-gather.4.cloned.1.call-done = bf16[384,5120]{0,1:T(8,128)(2,1)} async-done(((bf16[384,320]{0,1:T(8,128)(2,1)}), bf16[384,5120]{0,1:T(8,128)(2,1)}) %all-gather.4.cloned.1.call-update) | async-done | bytes 3932176 | tf_op jit(solution)/shard_map/all_gather | solution.py:107
  61.9 8.0 %convolution_convert_fusion.1 = bf16[576,5120]{1,0:T(8,128)(2,1)} fusion(bf16[576,384]{1,0:T(8,128)(2,1)} %param.14, bf16[384,5120]{0,1:T(8,128)(2,1)} %all-gather.4.cloned.1.call-done), kind=kOutput, calls=%fused_computation.13 | convolution fusion | flops 2267873280 | bytes 10272768 | tf_op jit(solution)/shard_map/dot_general | solution.py:105
  69.9 8.8 %copy.34 = bf16[576,5120]{0,1:T(8,128)(2,1)} copy(bf16[576,5120]{1,0:T(8,128)(2,1)} %convolution_convert_fusion.1) | data formatting | bytes 11796480
  78.8 0.7 all-gather.6.cloned.1.call-update
  79.6 0.5 all-gather.8.cloned.1.call-update
  80.8 0.6 dynamic_slice.15
  81.4 0.6 add_minimum_fusion
  82.8 20.7 %psum.14 = bf16[576,16]{0,1:T(8,128)(2,1)S(1)} all-reduce(bf16[576,16]{0,1:T(8,128)(2,1)S(1)} %fusion.18), channel_id=1, replica_groups=mesh['req'=16,'mlp'=8] {'mlp'}, use_global_device_ids=true, to_apply=%region_10.11 | all-reduce | flops 9216 | bytes 36864 | tf_op jit(solution)/shard_map/psum | solution.py:118
  103.5 18.3 %reduce-scatter.7.cloned.1.call-done = bf16[640,576]{1,0:T(8,128)(2,1)} async-done(((bf16[5120,576]{1,0:T(8,128)(2,1)}), bf16[640,576]{1,0:T(8,128)(2,1)}) %reduce-scatter.7.cloned.1.call-update) | async-done | bytes 737296
  121.8 1.5 copy.35
  123.3 3.2 broadcast_in_dim.79
  126.5 1.4 constant_dynamic-update-slice_fusion.7
  127.9 0.6 collective-permute-start
  128.5 8.4 %collective-permute-done = bf16[576,640]{1,0:T(8,128)(2,1)S(1)} collective-permute-done((bf16[576,640]{1,0:T(8,128)(2,1)S(1)}, bf16[576,640]{1,0:T(8,128)(2,1)S(1)}, u32[]{:S(2)}, u32[]{:S(2)}) %collective-permute-start) | collective-permute-done | bytes 737312 | tf_op jit(solution)/shard_map/ppermute | solution.py:22
  136.9 2.5 collective-permute-start.2
  139.4 0.4 collective-permute-done.1
  139.8 8.0 %collective-permute-done.2 = bf16[576,640]{1,0:T(8,128)(2,1)} collective-permute-done((bf16[576,640]{1,0:T(8,128)(2,1)S(1)}, bf16[576,640]{1,0:T(8,128)(2,1)}, u32[]{:S(2)}, u32[]{:S(2)}) %collective-permute-start.2) | collective-permute-done | bytes 737312 | tf_op jit(solution)/shard_map/ppermute | solution.py:22
  147.8 2.6 collective-permute-start.4
  150.3 0.7 collective-permute-done.3
  151.1 18.2 %fusion.22 = f32[576,3,5120]{2,0,1:T(8,128)} fusion(f32[8,3,5120]{2,0,1:T(8,128)S(1)} %copy-done, s32[576]{0:T(1024)S(1)} %select_reduce_fusion), kind=kOutput, calls=%fused_computation.38 | convolution fusion | flops 849351168 | bytes 35883264 | tf_op jit(solution)/shard_map/dot_general | solution.py:61
  169.2 1.7 collective-permute-start.6
  171.0 1.0 constant_dynamic-update-slice_fusion.6
  172.0 1.0 constant_dynamic-update-slice_fusion.5
  173.0 2.1 constant_dynamic-update-slice_fusion.4
  175.1 1.0 constant_dynamic-update-slice_fusion.3
  176.1 1.0 constant_dynamic-update-slice_fusion.2
  177.1 2.1 constant_dynamic-update-slice_fusion.1
  179.4 1.0 constant_dynamic-update-slice_fusion
  180.3 4.7 %convert_reduce_fusion = (f32[576]{0:T(1024)S(1)}, f32[576]{0:T(1024)S(1)}) fusion(bf16[576,5120]{1,0:T(8,128)(2,1)} %constant_dynamic-update-slice_fusion), kind=kLoop, calls=%fused_computation.3 | loop fusion | flops 11795328 | bytes 5902848 | tf_op jit(solution)/shard_map/reduce_sum | solution.py:131
  185.0 11.4 %fusion.3 = bf16[576,5120]{1,0:T(8,128)(2,1)S(1)} fusion(bf16[576,5120]{1,0:T(8,128)(2,1)} %constant_dynamic-update-slice_fusion, f32[576,3,5120]{2,0,1:T(8,128)} %fusion.22, f32[576]{0:T(1024)S(1)} %get-tuple-element.8, f32[576]{0:T(1024)S(1)} %get-tuple-element.7), kind=kLoop, calls=%fused_computation.7 | loop fusion | flops 20643840 | bytes 35394048 | tf_op jit(solution)/shard_map/convert_element_type | solution.py:138
  196.4 2.5 copy-done.2
  198.9 0.5 fusion.17
  199.4 26.8 %psum.15 = bf16[576,16]{0,1:T(8,128)(2,1)S(1)} all-reduce(bf16[576,16]{0,1:T(8,128)(2,1)S(1)} %fusion.17), channel_id=1, replica_groups=mesh['req'=16,'mlp'=8] {'mlp'}, use_global_device_ids=true, to_apply=%region_14.15 | all-reduce | flops 9216 | bytes 36864 | tf_op jit(solution)/shard_map/psum | solution.py:147
  226.2 0.5 fusion.26
  226.7 12.1 %fusion.13 = bf16[576,864]{1,0:T(8,128)(2,1)} fusion(f32[576,864,1]{1,0,2:T(8,128)S(1)} %fusion.26, bf16[576,5120]{1,0:T(8,128)(2,1)} %copy-done.2, bf16[5120,864]{1,0:T(8,128)(2,1)} %all-gather.6.cloned.1.call-done), kind=kOutput, calls=%fused_computation.22 | convolution fusion | flops 5101056000 | bytes 17731584 | tf_op jit(solution)/shard_map/dot_general | solution.py:149
  238.8 36.4 %all-gather.8.cloned.1.call-done = bf16[864,5120]{0,1:T(8,128)(2,1)} async-done(((bf16[864,320]{0,1:T(8,128)(2,1)}), bf16[864,5120]{0,1:T(8,128)(2,1)}) %all-gather.8.cloned.1.call-update) | async-done | bytes 8847376 | tf_op jit(solution)/shard_map/all_gather | solution.py:162
  275.2 10.7 %convolution_convert_fusion = bf16[576,5120]{1,0:T(8,128)(2,1)} fusion(bf16[576,864]{1,0:T(8,128)(2,1)} %fusion.13, bf16[864,5120]{0,1:T(8,128)(2,1)} %all-gather.8.cloned.1.call-done), kind=kOutput, calls=%fused_computation.12 | convolution fusion | flops 5099028480 | bytes 15740928 | tf_op jit(solution)/shard_map/dot_general | solution.py:160
  285.9 8.6 %copy.36 = bf16[576,5120]{0,1:T(8,128)(2,1)} copy(bf16[576,5120]{1,0:T(8,128)(2,1)} %convolution_convert_fusion) | data formatting | bytes 11796480
  294.5 10.4 %slice.14 = f32[576,1,5120]{2,0,1:T(8,128)} slice(f32[576,3,5120]{2,0,1:T(8,128)} %fusion.22), slice={[0:576], [2:3], [0:5120]} | slice | bytes 23592960 | tf_op jit(solution)/shard_map/slice | solution.py:103
  306.8 30.5 %reduce-scatter.9.cloned.1.call-done = bf16[640,576]{1,0:T(8,128)(2,1)} async-done(((bf16[5120,576]{1,0:T(8,128)(2,1)}), bf16[640,576]{1,0:T(8,128)(2,1)}) %reduce-scatter.9.cloned.1.call-update) | async-done | bytes 737296
  337.3 1.5 copy.37
  338.8 1.6 fusion.15
  340.6 1.3 fusion.19
  341.8 6.7 %all-to-all-start = ((bf16[36,16,640]{2,0,1:T(8,128)(2,1)}), bf16[36,16,640]{2,0,1:T(8,128)(2,1)S(1)}, u32[]{:S(2)}, u32[]{:S(2)}) async-start(bf16[36,16,640]{2,0,1:T(8,128)(2,1)} %fusion.19), calls=%async_computation | async-start | bytes 1638400 | tf_op jit(solution)/shard_map/all_to_all | solution.py:208
  348.8 16.5 %all-to-all-done = bf16[36,16,640]{2,0,1:T(8,128)(2,1)S(1)} async-done(((bf16[36,16,640]{2,0,1:T(8,128)(2,1)}), bf16[36,16,640]{2,0,1:T(8,128)(2,1)S(1)}, u32[]{:S(2)}, u32[]{:S(2)}) %all-to-all-start) | async-done | bytes 737312 | tf_op jit(solution)/shard_map/all_to_all | solution.py:208
  365.3 2.2 gather_fusion
  367.5 0.9 bitcast_select_fusion
  (65 shorter events, 2.2 us)
Async XLA Ops:
  6.5 144.5 %copy-start = (f32[8,3,5120]{2,0,1:T(8,128)S(1)}, f32[8,3,5120]{2,0,1:T(8,128)}, u32[]{:S(2)}) copy-start(f32[8,3,5120]{2,0,1:T(8,128)} %param.21) | copy-start | bytes 1474564
  6.5 55.4 %all-gather.4.cloned.1.call-start = ((), (), s32[]{:S(2)}) async-start(), calls=%async_computation.3 | async-start | bytes 4177920 | tf_op jit(solution)/shard_map/all_gather | solution.py:107
  7.3 114.5 %reduce-scatter.7.cloned.1.call-start = ((), (), s32[]{:S(2)}) async-start(), calls=%async_computation.6 | async-start | bytes 7372800
  78.7 1.4 copy-start.5
  78.7 3.4 copy-start.6
  78.7 3.6 copy-start.7
  78.7 3.7 copy-start.10
  78.7 3.7 copy-start.13
  78.8 47.7 %copy-start.8 = (bf16[576,640]{1,0:T(8,128)(2,1)S(1)}, bf16[576,640]{1,0:T(8,128)(2,1)}, u32[]{:S(2)}) copy-start(bf16[576,640]{1,0:T(8,128)(2,1)} %param.13) | copy-start | bytes 2211844
  78.8 47.7 %copy-start.11 = (bf16[16,16,640]{2,1,0:T(8,128)(2,1)S(1)}, bf16[16,16,640]{2,1,0:T(8,128)(2,1)}, u32[]{:S(2)}) copy-start(bf16[16,16,640]{2,1,0:T(8,128)(2,1)} %param.20) | copy-start | bytes 983044
  78.8 147.9 %all-gather.6.cloned.1.call-start = ((), (), s32[]{:S(2)}) async-start(), calls=%async_computation.4 | async-start | bytes 9748480 | tf_op jit(solution)/shard_map/all_gather | solution.py:151
  79.5 195.6 %all-gather.8.cloned.1.call-start = ((), (), s32[]{:S(2)}) async-start(), calls=%async_computation.5 | async-start | bytes 9748480 | tf_op jit(solution)/shard_map/all_gather | solution.py:162
  80.1 257.2 %reduce-scatter.9.cloned.1.call-start = ((), (), s32[]{:S(2)}) async-start(), calls=%async_computation.7 | async-start | bytes 7372800
  127.9 23.1 %copy-start.3 = (bf16[576,640]{1,0:T(8,128)(2,1)}, bf16[576,640]{1,0:T(8,128)(2,1)S(1)}, u32[]{:S(2)}) copy-start(bf16[576,640]{1,0:T(8,128)(2,1)S(1)} %get-tuple-element.12) | copy-start | bytes 2211844
  127.9 9.0 %collective-permute-start = (bf16[576,640]{1,0:T(8,128)(2,1)S(1)}, bf16[576,640]{1,0:T(8,128)(2,1)S(1)}, u32[]{:S(2)}, u32[]{:S(2)}) collective-permute-start(bf16[576,640]{1,0:T(8,128)(2,1)S(1)} %get-tuple-element.12), channel_id=1, source_target_pairs={{0,1},{1,2},{2,3},{3,4},{4,5},{5,6},{6,7},{7,0},{8,9},{9,10},{10,1... | collective-permute-start | bytes 2211848 | tf_op jit(solution)/shard_map/ppermute | solution.py:22
  128.5 11.3 %collective-permute-start.1 = (bf16[576,640]{1,0:T(8,128)(2,1)S(1)}, bf16[576,640]{1,0:T(8,128)(2,1)S(1)}, u32[]{:S(2)}, u32[]{:S(2)}) collective-permute-start(bf16[576,640]{1,0:T(8,128)(2,1)S(1)} %get-tuple-element.12), channel_id=1, source_target_pairs={{0,7},{1,0},{2,1},{3,2},{4,3},{5,4},{6,5},{7,6},{8,15},{9,8},{10,9... | collective-permute-start | bytes 2211848 | tf_op jit(solution)/shard_map/ppermute | solution.py:25
  136.9 10.9 %collective-permute-start.2 = (bf16[576,640]{1,0:T(8,128)(2,1)S(1)}, bf16[576,640]{1,0:T(8,128)(2,1)}, u32[]{:S(2)}, u32[]{:S(2)}) collective-permute-start(bf16[576,640]{1,0:T(8,128)(2,1)S(1)} %collective-permute-done), channel_id=1, source_target_pairs={{0,1},{1,2},{2,3},{3,4},{4,5},{5,6},{6,7},{7,0},{8,9},{9,10},{10,1... | collective-permute-start | bytes 2211848 | tf_op jit(solution)/shard_map/ppermute | solution.py:22
  139.8 11.3 %collective-permute-start.3 = (bf16[576,640]{1,0:T(8,128)(2,1)S(1)}, bf16[576,640]{1,0:T(8,128)(2,1)S(1)}, u32[]{:S(2)}, u32[]{:S(2)}) collective-permute-start(bf16[576,640]{1,0:T(8,128)(2,1)S(1)} %collective-permute-done.1), channel_id=1, source_target_pairs={{0,7},{1,0},{2,1},{3,2},{4,3},{5,4},{6,5},{7,6},{8,15},{9,8},{10,9... | collective-permute-start | bytes 2211848 | tf_op jit(solution)/shard_map/ppermute | solution.py:25
  147.8 21.5 %collective-permute-start.4 = (bf16[576,640]{1,0:T(8,128)(2,1)}, bf16[576,640]{1,0:T(8,128)(2,1)S(1)}, u32[]{:S(2)}, u32[]{:S(2)}) collective-permute-start(bf16[576,640]{1,0:T(8,128)(2,1)} %collective-permute-done.2), channel_id=1, source_target_pairs={{0,1},{1,2},{2,3},{3,4},{4,5},{5,6},{6,7},{7,0},{8,9},{9,10},{10,1... | collective-permute-start | bytes 2211848 | tf_op jit(solution)/shard_map/ppermute | solution.py:22
  151.0 26.1 %collective-permute-start.5 = (bf16[576,640]{1,0:T(8,128)(2,1)S(1)}, bf16[576,640]{1,0:T(8,128)(2,1)}, u32[]{:S(2)}, u32[]{:S(2)}) collective-permute-start(bf16[576,640]{1,0:T(8,128)(2,1)S(1)} %collective-permute-done.3), channel_id=1, source_target_pairs={{0,7},{1,0},{2,1},{3,2},{4,3},{5,4},{6,5},{7,6},{8,15},{9,8},{10,9... | collective-permute-start | bytes 2211848 | tf_op jit(solution)/shard_map/ppermute | solution.py:25
  169.2 10.1 %collective-permute-start.6 = (bf16[576,640]{1,0:T(8,128)(2,1)S(1)}, bf16[576,640]{1,0:T(8,128)(2,1)S(1)}, u32[]{:S(2)}, u32[]{:S(2)}) collective-permute-start(bf16[576,640]{1,0:T(8,128)(2,1)S(1)} %collective-permute-done.4), channel_id=1, source_target_pairs={{0,1},{1,2},{2,3},{3,4},{4,5},{5,6},{6,7},{7,0},{8,9},{9,10},{10,1... | collective-permute-start | bytes 2211848 | tf_op jit(solution)/shard_map/ppermute | solution.py:22
  185.0 13.9 %copy-start.12 = (bf16[640,16,16]{0,2,1:T(8,128)(2,1)S(1)}, bf16[640,16,16]{0,2,1:T(8,128)(2,1)}, u32[]{:S(2)}) copy-start(bf16[640,16,16]{0,2,1:T(8,128)(2,1)} %param.22) | copy-start | bytes 983044
  185.0 41.1 %copy-start.9 = (bf16[16,16,864]{2,1,0:T(8,128)(2,1)S(1)}, bf16[16,16,864]{2,1,0:T(8,128)(2,1)}, u32[]{:S(2)}) copy-start(bf16[16,16,864]{2,1,0:T(8,128)(2,1)} %param.23) | copy-start | bytes 1327108
  196.4 2.5 copy-start.2
  294.5 44.3 %copy-start.4 = (bf16[576,640]{1,0:T(8,128)(2,1)S(1)}, bf16[576,640]{1,0:T(8,128)(2,1)}, u32[]{:S(2)}) copy-start(bf16[576,640]{1,0:T(8,128)(2,1)} %copy-done.3) | copy-start | bytes 2211844
  340.4 28.1 %copy-start.1 = (f32[8,3,5120]{2,0,1:T(8,128)S(1)}, f32[8,3,5120]{2,0,1:T(8,128)}, u32[]{:S(2)}) copy-start(f32[8,3,5120]{2,0,1:T(8,128)} %param.21) | copy-start | bytes 1474564
  341.8 23.4 %all-to-all-start = ((bf16[36,16,640]{2,0,1:T(8,128)(2,1)}), bf16[36,16,640]{2,0,1:T(8,128)(2,1)S(1)}, u32[]{:S(2)}, u32[]{:S(2)}) async-start(bf16[36,16,640]{2,0,1:T(8,128)(2,1)} %fusion.19), calls=%async_computation | async-start | bytes 1638400 | tf_op jit(solution)/shard_map/all_to_all | solution.py:208
Sparse Core Ops, SparseCore 0:
  9.5 52.4 all-gather.3
  78.9 42.8 reduce-scatter.6
  123.9 75.1 all-gather.5
  201.1 74.0 all-gather.7
  294.6 42.6 reduce-scatter.8
